TPU v7x, 256 devices: a whole 4x4x8 slice. The times are simulated.
256 devices in a mesh: seq: 32 (over z, y), dp: 8 (over x, core).
Axes of the slice: x: 4, y: 4, z: 8, core: 2. Of those that a mesh axis runs over, the one named last changes fastest.
Arguments:
- queries: bfloat16 [8, 12288, 2048], P('dp', 'seq'), may hold values from -0.59765625 to 0.59765625
- keys: bfloat16 [8, 12288, 2048], P('dp', 'seq'), may hold values from -0.59765625 to 0.59765625
- values: bfloat16 [8, 12288, 2048], P('dp', 'seq'), may hold values from -6 to 6
- output_gradient: bfloat16 [8, 12288, 2048], P('dp', 'seq'), may hold values from -0.59765625 to 0.59765625
- document_lengths: int32 [8, 8], P('dp'), may hold values from 1 to 3072, 12288 in all within a row
- cutoff_rows: int32 [8, 12288], P('dp', 'seq'), may hold values 0 or 1
- head_decay_rate: float32 [16], replicated, may hold values from 4.06901042e-06 to 0.04, as said below
Outputs:
- query_grad: bfloat16 [8, 12288, 2048], P('dp', 'seq')
- key_grad: bfloat16 [8, 12288, 2048], P('dp', 'seq')
- value_grad: bfloat16 [8, 12288, 2048], P('dp', 'seq')
- rate_grad: float32 [16], replicated
Inputs may be any that keep to these rules, and one draw needn't show every extreme that they name: `head_decay_rate`: a positive rate for each head.
All inputs are finite; a program needn't handle non-finite values. No bound on the sum of `cutoff_rows` on one device may be relied on, other than what follows from the above.
Results may differ from a plain program's by a relative error of at most 0.0034.
Values sent between devices are 32-bit elements; how exact they have to be, the bound alone decides.
No kernel may reach another device: no remote copies, remote signals or barrier semaphores. Data moves between devices by JAX's collectives and lax.ppermute only.
A program may use at most 192 MiB of HBM per device.

v0:
```python
import math
import jax
import jax.numpy as jnp
from jax import lax
from jax.sharding import PartitionSpec as P

HEADS = 16
HEAD_DIM = 128
cutoff_logarithm = math.log(0.7)
state_mode = lax.Precision.HIGH


def carried_in(part, axis, combine, identity, reverse):
    count = lax.axis_size(axis)
    place = lax.axis_index(axis)
    ahead = count - 1 - place if reverse else place
    gathered = jax.tree.map(lambda a: lax.all_gather(a, axis), part)
    state = jax.tree.map(lambda a, e: jnp.zeros_like(a) + jnp.asarray(e, a.dtype), part, identity)

    def one(step, state):
        source = count - 1 - step if reverse else step
        return combine(
            state, jax.tree.map(lambda a: lax.dynamic_index_in_dim(a, source, 0, False), gathered)
        )

    return lax.fori_loop(0, ahead, one, state)


def block_mask_list(head_decay_rate, cutoff_list, row_position, start_list):
    is_start = jnp.any(row_position[:, None] == start_list[None, :], axis=1)
    seg_local = jnp.cumsum(is_start.astype(jnp.int32))
    begin = jnp.max(
        jnp.where(start_list[None, :] <= row_position[:, None], start_list[None, :], 0), axis=1
    )
    position = (row_position - begin).astype(jnp.float32)
    logarithm_step = (
        cutoff_list.astype(jnp.float32)[:, None] * cutoff_logarithm - head_decay_rate[None, :]
    )
    cum_log = jnp.cumsum(logarithm_step, axis=0)
    carry_in = jnp.where((seg_local == 0)[:, None], jnp.exp(cum_log), 0.0)
    carry_out = jnp.where(
        (seg_local == seg_local[-1])[:, None], jnp.exp(cum_log[-1][None, :] - cum_log), 0.0
    )
    decay_all = jnp.where(seg_local[-1] == 0, jnp.exp(cum_log[-1]), 0.0)
    return (cum_log, seg_local, position, carry_in, carry_out, decay_all)


def weights_of(cum_log, seg_local):
    count = seg_local.shape[0]
    index = jnp.arange(count, dtype=jnp.int32)
    allowed = (seg_local[:, None] == seg_local[None, :]) & (index[:, None] >= index[None, :])
    spread = cum_log.T[:, :, None] - cum_log.T[:, None, :]
    return jnp.where(allowed[None], jnp.exp(jnp.where(allowed[None], spread, 0.0)), 0.0)


def forward_combine(earlier, later):
    return (earlier[0] * later[0], later[0][:, None, None] * earlier[1] + later[1])


def backward_combine(earlier, later):
    return (later[0] * earlier[0], later[1] + later[0][:, None, None] * earlier[1])


def on_device(
    queries, keys, values, output_gradient, document_lengths, cutoff_rows, head_decay_rate
):
    row_count = queries.shape[1]
    query_block = queries.reshape(row_count, HEADS, HEAD_DIM)
    key_block = keys.reshape(row_count, HEADS, HEAD_DIM)
    value_block = values.reshape(row_count, HEADS, HEAD_DIM)
    gradient_block = output_gradient.reshape(row_count, HEADS, HEAD_DIM)
    block_piece = lax.axis_index("seq")
    row_position = block_piece * row_count + jnp.arange(row_count, dtype=jnp.int32)
    length_list = document_lengths[0]
    start_list = jnp.cumsum(length_list) - length_list
    cum_log, seg_local, position, carry_in, carry_out, decay_all = block_mask_list(
        head_decay_rate, cutoff_rows[0], row_position, start_list
    )
    key_f = key_block.astype(jnp.float32)
    value_f = value_block.astype(jnp.float32)
    grad_f = gradient_block.astype(jnp.float32)
    query_f = query_block.astype(jnp.float32)
    state_local = jnp.einsum(
        "the,thf->hef", carry_out[:, :, None] * key_f, value_f, precision=state_mode
    )
    back_local = jnp.einsum(
        "she,shf->hef", carry_in[:, :, None] * query_f, grad_f, precision=state_mode
    )
    identity = (jnp.ones_like(decay_all), jnp.zeros_like(state_local))
    state_input = carried_in((decay_all, state_local), "seq", forward_combine, identity, False)[1]
    backward_input = carried_in((decay_all, back_local), "seq", backward_combine, identity, True)[1]
    weight = weights_of(cum_log, seg_local)
    scores = jnp.einsum("she,the->hst", query_block, key_block, preferred_element_type=jnp.float32)
    grad_scores = jnp.einsum(
        "shf,thf->hst", gradient_block, value_block, preferred_element_type=jnp.float32
    )
    attn_prob = (weight * scores).astype(jnp.bfloat16)
    grad_prob = (weight * grad_scores).astype(jnp.bfloat16)
    value_full = jnp.einsum(
        "hst,shf->thf", attn_prob, gradient_block, preferred_element_type=jnp.float32
    )
    value_full = value_full + carry_out[:, :, None] * jnp.einsum(
        "the,hef->thf", key_f, backward_input, precision=state_mode
    )
    query_full = jnp.einsum(
        "hst,the->she", grad_prob, key_block, preferred_element_type=jnp.float32
    )
    query_full = query_full + carry_in[:, :, None] * jnp.einsum(
        "shf,hef->she", grad_f, state_input, precision=state_mode
    )
    key_full = jnp.einsum(
        "hst,she->the", grad_prob, query_block, preferred_element_type=jnp.float32
    )
    key_full = key_full + carry_out[:, :, None] * jnp.einsum(
        "thf,hef->the", value_f, backward_input, precision=state_mode
    )
    inner_step = jnp.sum(key_f * key_full, axis=2) - jnp.sum(query_f * query_full, axis=2)
    rate_part = jnp.sum(position[:, None] * inner_step, axis=0)
    rate_total = lax.psum(rate_part, ("seq", "dp"))
    token_total = row_count * lax.axis_size("seq") * lax.axis_size("dp")
    rate_grad = head_decay_rate * rate_total / math.sqrt(token_total)
    out_shape = (1, row_count, HEADS * HEAD_DIM)
    return (
        query_full.astype(jnp.bfloat16).reshape(out_shape),
        key_full.astype(jnp.bfloat16).reshape(out_shape),
        value_full.astype(jnp.bfloat16).reshape(out_shape),
        rate_grad,
    )


def solution(mesh):
    in_specs = (
        P("dp", "seq", None),
        P("dp", "seq", None),
        P("dp", "seq", None),
        P("dp", "seq", None),
        P("dp", None),
        P("dp", "seq"),
        P(),
    )
    out_specs = (P("dp", "seq", None), P("dp", "seq", None), P("dp", "seq", None), P())
    return jax.shard_map(
        on_device, mesh=mesh, in_specs=in_specs, out_specs=out_specs, check_vma=False
    )
```

profile of v0, /device:TPU:1, one launch (start us, length us, event | category | flops | bytes accessed | tf_op | source)
XLA Modules:
  0.0 647.6 jit_solution(15343796747295576941)
XLA Ops:
  13.9 1.9 copy.84
  15.8 2.4 copy.99
  18.5 2.4 fusion.9
  21.0 1.9 copy.81
  22.8 1.8 copy.101
  25.8 2.4 fusion.7
  28.2 38.4 %all-gather.2 = f32[32,1,16]{2,1,0:T(1,128)S(1)} all-gather(f32[1,1,16]{2,1,0:T(1,128)S(1)} %bitcast.115), channel_id=1, replica_groups=mesh['seq'=32,'dp'=8] {'seq'}, dimensions={0}, use_global_device_ids=true | all-gather | bytes 2112 | tf_op jit(solution)/shard_map/all_gather | solution.py:17
  66.9 6.9 %multiply_convert_fusion.1 = bf16[16,384,384]{2,1,0:T(8,128)(2,1)} fusion(f32[16,384]{1,0:T(8,128)S(1)} %get-tuple-element.184, pred[384,384]{1,0:T(8,128)(4,1)S(1)} %fusion.21, bf16[384,16,128]{0,2,1:T(8,128)(2,1)S(1)} %bitcast.99, bf16[384,16,128]{2,1,0:T(8,128)(2,1)} %bitcast.103), kind=kOutput, calls=%fused_computation.5 | convolution fusion | flops 615776256 | bytes 8036352 | tf_op jit(solution)/shard_map/shf,thf->hst/dot_general | solution.py:94
  73.8 184.0 %all-gather.8.cloned.1.call-done = f32[512,128,128]{2,1,0:T(8,128)} async-done(((f32[16,128,128]{2,1,0:T(8,128)}), f32[512,128,128]{2,1,0:T(8,128)}) %all-gather.8.cloned.1.call-update) | async-done | bytes 33554448 | tf_op jit(solution)/shard_map/all_gather | solution.py:17
  257.9 46.7 %while.27 = (s32[]{:T(128)}, f32[16,128,128]{2,1,0:T(8,128)S(1)}, s32[]{:T(128)}, f32[32,16,128,128]{3,2,1,0:T(8,128)}, f32[32,16]{1,0:T(8,128)S(1)}, /*index=5*/s32[]{:T(128)}, s32[]{:T(128)}, s32[]{:T(128)}, s32[]{:T(128)}) while((s32[]{:T(128)}, f32[16,128,128]{2,1,0:T(8,128)S(1)}, s32[]{:T(128)}, f32[32,16,128,128]{3,2,1,0:T(8,128)}, ...), condition=%wide.region_9.10_spmd, body=%wide.region_8.9_spmd.sunk | while | flops 524294 | bytes 3146075 | solution.py:26
  269.9 1.6 bitcast_add_fusion.5
  271.5 1.5 bitcast_add_fusion.5
  280.6 1.5 bitcast_add_fusion.5
  304.6 4.5 fusion.17
  309.2 2.7 fusion.25
  311.8 178.9 %all-gather.6.cloned.1.call-done = f32[512,128,128]{2,1,0:T(8,128)} async-done(((f32[16,128,128]{2,1,0:T(8,128)}), f32[512,128,128]{2,1,0:T(8,128)}) %all-gather.6.cloned.1.call-update) | async-done | bytes 33554448 | tf_op jit(solution)/shard_map/all_gather | solution.py:17
  491.1 4.0 fusion.24
  495.1 8.2 %fusion.12 = bf16[384,16,128]{0,2,1:T(8,128)(2,1)} fusion(f32[16,128,384]{2,1,0:T(8,128)} %fusion.25, bf16[384,16,128]{0,2,1:T(8,128)(2,1)} %bitcast.101, f32[16,384]{1,0:T(8,128)S(1)} %get-tuple-element.184, pred[384,384]{1,0:T(8,128)(4,1)S(1)} %fusion.21, bf16[384,16,128]{0,2,1:T(8,128)(2,1)} %bitcast.95, bf16[384,16,128]{0,2,1:T(8,128)(2,1)S(1)} %bitcast.91, ...), kind=kOutput, calls=%fused_computation.23 | convolution fusion | flops 1222115328 | bytes 9633792 | tf_op jit(solution)/shard_map/hst,shf->thf/dot_general | solution.py:99
  503.3 2.7 copy.94
  506.0 5.9 fusion.8
  512.0 5.1 fusion.10
  517.2 2.7 copy.92
  519.9 118.8 %psum.7 = f32[16]{0:T(128)S(1)} all-reduce(f32[16]{0:T(128)S(1)} %multiply_reduce_fusion), channel_id=1, replica_groups=mesh['seq'=32,'dp'=8] {'seq','dp'}, use_global_device_ids=true, to_apply=%region_14.15 | all-reduce | flops 16 | bytes 128 | tf_op jit(solution)/shard_map/psum | solution.py:119
  639.2 1.6 copy.93
  (105 shorter events, 49.9 us)
Async XLA Ops:
  7.2 250.6 %all-gather.8.cloned.1.call-start = ((), (), s32[]{:S(2)}) async-start(), calls=%async_computation.1 | async-start | bytes 34603008 | tf_op jit(solution)/shard_map/all_gather | solution.py:17
  15.8 5.1 copy-start
  18.2 48.7 %copy-start.2 = (bf16[1,384,2048]{1,2,0:T(8,128)(2,1)}, bf16[1,384,2048]{1,2,0:T(8,128)(2,1)S(1)}, u32[]{:S(2)}) copy-start(bf16[1,384,2048]{1,2,0:T(8,128)(2,1)S(1)} %copy.99) | copy-start | bytes 4718596
  20.9 469.8 %all-gather.6.cloned.1.call-start = ((), (), s32[]{:S(2)}) async-start(), calls=%async_computation | async-start | bytes 34603008 | tf_op jit(solution)/shard_map/all_gather | solution.py:17
  24.7 1.1 copy-start.3
  503.3 2.7 copy-start.1
  506.0 5.9 copy-start.4
  517.1 121.6 %copy-start.6 = (f32[16]{0:T(128)S(1)}, f32[16]{0:T(128)}, u32[]{:S(2)}) copy-start(f32[16]{0:T(128)} %param.17) | copy-start | bytes 196
  517.1 122.1 %copy-start.5 = (bf16[384,16,128]{0,2,1:T(8,128)(2,1)S(1)}, bf16[384,16,128]{0,2,1:T(8,128)(2,1)}, u32[]{:S(2)}) copy-start(bf16[384,16,128]{0,2,1:T(8,128)(2,1)} %get-tuple-element.181) | copy-start | bytes 4718596
Sparse Core Ops, SparseCore 0:
  21.0 236.7 all-gather.7
  260.4 230.3 all-gather.5
where the time goes:
time: 649 us; the launch traced here: 648 us
  waiting for transfers between devices  363 us (56%)
  blocking collectives  157 us (24%)
  other arithmetic  51.5 us (8%)
  matrix products  42 us (6%)
  local copies, waits for them, and re-layouts  17.7 us (3%)
  between operations  14.8 us (2%)
    all_gather x2, waiting for transfers between devices, carried_in(): gathered = jax.tree.map(lambda a: lax.all_gather(a, axis), part)  363 us
    psum x1, blocking collectives, on_device(): rate_total = lax.psum(rate_part, ('seq', 'dp'))  119 us
    add x31, other arithmetic, backward_combine(): later[1] + later[0][:, None, None] * earlier[1]  45.3 us
    all_gather x1, blocking collectives, carried_in(): gathered = jax.tree.map(lambda a: lax.all_gather(a, axis), part)  38.4 us
    unnamed x20, local copies, waits for them, and re-layouts  13.7 us
  transfers between devices with their start and end apart: 2, of which 2 were waited for; matrix products, arithmetic and copies ran while one was open for 10% of the time, Pallas kernels for 0%

commit v1 on v0

--- a/solution.py
+++ b/solution.py
@@ -3,6 +3,7 @@
 import jax.numpy as jnp
 from jax import lax
 from jax.sharding import PartitionSpec as P
+from jax.lax import psum
 
 HEADS = 16
 HEAD_DIM = 128
@@ -116,7 +117,7 @@
     )
     inner_step = jnp.sum(key_f * key_full, axis=2) - jnp.sum(query_f * query_full, axis=2)
     rate_part = jnp.sum(position[:, None] * inner_step, axis=0)
-    rate_total = lax.psum(rate_part, ("seq", "dp"))
+    rate_total = psum(psum(rate_part, "seq"), "dp")
     token_total = row_count * lax.axis_size("seq") * lax.axis_size("dp")
     rate_grad = head_decay_rate * rate_total / math.sqrt(token_total)
     out_shape = (1, row_count, HEADS * HEAD_DIM)

time: 649 us -> 661 us (1.018)
  blocking collectives: 157 us -> 169 us
    psum x1 -> x2, blocking collectives: 119 us -> 130 us  [on_device(): rate_total = psum(psum(rate_part, 'seq'), 'dp')]
where the time goes in v1:
time: 661 us; the launch traced here: 659 us
  waiting for transfers between devices  363 us (55%)
  blocking collectives  169 us (26%)
  other arithmetic  51.5 us (8%)
  matrix products  42 us (6%)
  local copies, waits for them, and re-layouts  17.7 us (3%)
  between operations  14.8 us (2%)
    all_gather x2, waiting for transfers between devices, carried_in(): gathered = jax.tree.map(lambda a: lax.all_gather(a, axis), part)  363 us
    psum x2, blocking collectives, on_device(): rate_total = psum(psum(rate_part, 'seq'), 'dp')  130 us
    add x31, other arithmetic, backward_combine(): later[1] + later[0][:, None, None] * earlier[1]  45.3 us
    all_gather x1, blocking collectives, carried_in(): gathered = jax.tree.map(lambda a: lax.all_gather(a, axis), part)  38.4 us
    unnamed x20, local copies, waits for them, and re-layouts  13.7 us
  transfers between devices with their start and end apart: 2, of which 2 were waited for; matrix products, arithmetic and copies ran while one was open for 10% of the time, Pallas kernels for 0%

profile of v1, /device:TPU:1, one launch (start us, length us, event | category | flops | bytes accessed | tf_op | source)
XLA Modules:
  0.0 659.1 jit_solution(1694882951233286263)
XLA Ops:
  13.9 1.9 copy.84
  15.8 2.4 copy.99
  18.5 2.4 fusion.9
  21.0 1.9 copy.81
  22.8 1.8 copy.101
  25.8 2.4 fusion.7
  28.2 38.4 %all-gather.2 = f32[32,1,16]{2,1,0:T(1,128)S(1)} all-gather(f32[1,1,16]{2,1,0:T(1,128)S(1)} %bitcast.115), channel_id=1, replica_groups=mesh['seq'=32,'dp'=8] {'seq'}, dimensions={0}, use_global_device_ids=true | all-gather | bytes 2112 | tf_op jit(solution)/shard_map/all_gather | solution.py:18
  66.9 6.9 %multiply_convert_fusion.1 = bf16[16,384,384]{2,1,0:T(8,128)(2,1)} fusion(f32[16,384]{1,0:T(8,128)S(1)} %get-tuple-element.184, pred[384,384]{1,0:T(8,128)(4,1)S(1)} %fusion.21, bf16[384,16,128]{0,2,1:T(8,128)(2,1)S(1)} %bitcast.99, bf16[384,16,128]{2,1,0:T(8,128)(2,1)} %bitcast.103), kind=kOutput, calls=%fused_computation.5 | convolution fusion | flops 615776256 | bytes 8036352 | tf_op jit(solution)/shard_map/shf,thf->hst/dot_general | solution.py:95
  73.8 184.0 %all-gather.8.cloned.1.call-done = f32[512,128,128]{2,1,0:T(8,128)} async-done(((f32[16,128,128]{2,1,0:T(8,128)}), f32[512,128,128]{2,1,0:T(8,128)}) %all-gather.8.cloned.1.call-update) | async-done | bytes 33554448 | tf_op jit(solution)/shard_map/all_gather | solution.py:18
  257.9 46.7 %while.27 = (s32[]{:T(128)}, f32[16,128,128]{2,1,0:T(8,128)S(1)}, s32[]{:T(128)}, f32[32,16,128,128]{3,2,1,0:T(8,128)}, f32[32,16]{1,0:T(8,128)S(1)}, /*index=5*/s32[]{:T(128)}, s32[]{:T(128)}, s32[]{:T(128)}, s32[]{:T(128)}) while((s32[]{:T(128)}, f32[16,128,128]{2,1,0:T(8,128)S(1)}, s32[]{:T(128)}, f32[32,16,128,128]{3,2,1,0:T(8,128)}, ...), condition=%wide.region_9.10_spmd, body=%wide.region_8.9_spmd.sunk | while | flops 524294 | bytes 3146075 | solution.py:27
  269.9 1.6 bitcast_add_fusion.5
  271.5 1.5 bitcast_add_fusion.5
  304.6 4.5 fusion.17
  309.2 2.7 fusion.25
  311.8 178.9 %all-gather.6.cloned.1.call-done = f32[512,128,128]{2,1,0:T(8,128)} async-done(((f32[16,128,128]{2,1,0:T(8,128)}), f32[512,128,128]{2,1,0:T(8,128)}) %all-gather.6.cloned.1.call-update) | async-done | bytes 33554448 | tf_op jit(solution)/shard_map/all_gather | solution.py:18
  491.1 4.0 fusion.24
  495.1 8.2 %fusion.12 = bf16[384,16,128]{0,2,1:T(8,128)(2,1)} fusion(f32[16,128,384]{2,1,0:T(8,128)} %fusion.25, bf16[384,16,128]{0,2,1:T(8,128)(2,1)} %bitcast.101, f32[16,384]{1,0:T(8,128)S(1)} %get-tuple-element.184, pred[384,384]{1,0:T(8,128)(4,1)S(1)} %fusion.21, bf16[384,16,128]{0,2,1:T(8,128)(2,1)} %bitcast.95, bf16[384,16,128]{0,2,1:T(8,128)(2,1)S(1)} %bitcast.91, ...), kind=kOutput, calls=%fused_computation.23 | convolution fusion | flops 1222115328 | bytes 9633792 | tf_op jit(solution)/shard_map/hst,shf->thf/dot_general | solution.py:100
  503.3 2.7 copy.94
  506.0 5.9 fusion.8
  512.0 5.1 fusion.10
  517.2 2.7 copy.92
  519.9 103.5 %psum.14 = f32[16]{0:T(128)S(1)} all-reduce(f32[16]{0:T(128)S(1)} %multiply_reduce_fusion), channel_id=1, replica_groups=mesh['seq'=32,'dp'=8] {'seq'}, use_global_device_ids=true, to_apply=%region_14.15 | all-reduce | flops 16 | bytes 128 | tf_op jit(solution)/shard_map/psum | solution.py:120
  623.4 26.7 %psum.15 = f32[16]{0:T(128)S(1)} all-reduce(f32[16]{0:T(128)S(1)} %psum.14), channel_id=1, replica_groups=mesh['seq'=32,'dp'=8] {'dp'}, use_global_device_ids=true, to_apply=%region_15.16 | all-reduce | flops 16 | bytes 128 | tf_op jit(solution)/shard_map/psum | solution.py:120
  650.6 1.6 copy.93
  (106 shorter events, 51.4 us)
Async XLA Ops:
  7.2 250.6 %all-gather.8.cloned.1.call-start = ((), (), s32[]{:S(2)}) async-start(), calls=%async_computation.1 | async-start | bytes 34603008 | tf_op jit(solution)/shard_map/all_gather | solution.py:18
  15.8 5.1 copy-start
  18.2 48.7 %copy-start.2 = (bf16[1,384,2048]{1,2,0:T(8,128)(2,1)}, bf16[1,384,2048]{1,2,0:T(8,128)(2,1)S(1)}, u32[]{:S(2)}) copy-start(bf16[1,384,2048]{1,2,0:T(8,128)(2,1)S(1)} %copy.99) | copy-start | bytes 4718596
  20.9 469.8 %all-gather.6.cloned.1.call-start = ((), (), s32[]{:S(2)}) async-start(), calls=%async_computation | async-start | bytes 34603008 | tf_op jit(solution)/shard_map/all_gather | solution.py:18
  24.7 1.1 copy-start.3
  503.3 2.7 copy-start.1
  506.0 5.9 copy-start.4
  517.1 133.1 %copy-start.6 = (f32[16]{0:T(128)S(1)}, f32[16]{0:T(128)}, u32[]{:S(2)}) copy-start(f32[16]{0:T(128)} %param.17) | copy-start | bytes 196
  517.1 133.6 %copy-start.5 = (bf16[384,16,128]{0,2,1:T(8,128)(2,1)S(1)}, bf16[384,16,128]{0,2,1:T(8,128)(2,1)}, u32[]{:S(2)}) copy-start(bf16[384,16,128]{0,2,1:T(8,128)(2,1)} %get-tuple-element.181) | copy-start | bytes 4718596
Sparse Core Ops, SparseCore 0:
  21.0 236.7 all-gather.7
  260.4 230.3 all-gather.5
